TPU v7x, 128 devices: a whole 4x4x4 slice. The times are simulated.
128 devices in a mesh: gx: 8 (over x, core), yz: 16 (over z, y).
Axes of the slice: x: 4, y: 4, z: 4, core: 2. Of those that a mesh axis runs over, the one named last changes fastest.
Arguments:
- hidden_in: bfloat16 [2, 128, 8192], P(None, ('gx', 'yz')), may hold values from -6 to 6
- k_cache: bfloat16 [128, 1024, 1024], P(('gx', 'yz'))
- v_cache: bfloat16 [128, 1024, 1024], P(('gx', 'yz')), may hold values from -6 to 6
- lengths: int32 [128], P(('gx', 'yz')), may hold values from 1 to 1024, as said below
- counts: int32 [128, 16], P(('gx', 'yz')), may hold values from 0 to 3
- token_elem: int32 [512], replicated, may hold values from 0 to 16, as said below
- tokens: int32 [128], P(('gx', 'yz')), may hold values from 0 to 511
- attn_gain: float32 [8192], replicated, may hold values from 0.5 to 1.5
- qkv_weight: bfloat16 [8192, 10240], P('gx', 'yz'), may hold values from -0.0625 to 0.0625
- o_weight: bfloat16 [8192, 8192], P('gx', 'yz'), may hold values from -0.0625 to 0.0625
- ffn_gain: float32 [8192], replicated, may hold values from 0.5 to 1.5
- gate_up_weight: bfloat16 [8192, 57344], P('gx', 'yz'), may hold values from -0.0625 to 0.0625
- down_weight: bfloat16 [28672, 8192], P('gx', 'yz'), may hold values from -0.03125 to 0.03125
- final_gain: float32 [8192], replicated, may hold values from 0.5 to 1.5
- lm_weight: bfloat16 [8192, 512], P(('gx', 'yz'))
Outputs:
- layer_out: bfloat16 [2, 128, 8192], P(None, ('gx', 'yz'))
- log_probs: float32 [2, 128, 512], P(None, ('gx', 'yz'))
Inputs may be any that keep to these rules, and one draw needn't show every extreme that they name: `lengths`: some spectrum uses all 1024 positions. `token_elem`: some token has no element (value 16).
All inputs are finite; a program needn't handle non-finite values.
Results may differ from a plain program's by a relative error of at most 0.022.
Values may be sent and summed in bfloat16 or wider, within the bound.
No kernel may reach another device: no remote copies, remote signals or barrier semaphores. Data moves between devices by JAX's collectives and lax.ppermute only.
A program may use at most 128 MiB of HBM per device.

v0:
```python
import math
import jax
import jax.numpy as jnp
from jax import lax
from jax.sharding import PartitionSpec as P

FF = 28672
HEADS = 64
KV_HEADS = 8
HEAD = 128
VOCAB = 512
ELEMENTS = 16
NORM_EPS = 1e-05
ROPE_THETA = 500000.0


def norm_rows(values, gain_vec):
    wide = values.astype(jnp.float32)
    inverse = lax.rsqrt(jnp.mean(wide * wide, axis=-1, keepdims=True) + NORM_EPS)
    return (wide * inverse * gain_vec).astype(jnp.bfloat16)


def rotate(heads_in, positions):
    half_width = heads_in.shape[-1] // 2
    frequency = jnp.power(
        ROPE_THETA, -(jnp.arange(half_width, dtype=jnp.float32) * 2.0 / heads_in.shape[-1])
    )
    angles = positions.astype(jnp.float32)[:, None] * frequency[None, :]
    cos_part = jnp.cos(angles)[:, None, :]
    sin_part = jnp.sin(angles)[:, None, :]
    wide = heads_in.astype(jnp.float32)
    first_half = wide[..., :half_width]
    second_half = wide[..., half_width:]
    joined = jnp.concatenate(
        [
            first_half * cos_part - second_half * sin_part,
            second_half * cos_part + first_half * sin_part,
        ],
        -1,
    )
    return joined.astype(jnp.bfloat16)


def spread_rows(inputs):
    gathered = lax.all_gather(inputs, "yz", axis=0, tiled=True)
    return lax.all_to_all(gathered, "gx", split_axis=1, concat_axis=0, tiled=True)


def project(inputs, weight):
    spread = spread_rows(inputs)
    summed = lax.psum_scatter(
        jnp.dot(spread, weight, preferred_element_type=jnp.float32),
        "gx",
        scatter_dimension=0,
        tiled=True,
    )
    return lax.all_to_all(
        summed.astype(jnp.bfloat16), "yz", split_axis=0, concat_axis=1, tiled=True
    )


def head_logits(normed, lm_weight):
    slice_width = lm_weight.shape[0]
    offset_cols = lax.axis_index("yz") * slice_width
    spread = spread_rows(normed)
    own_cols = lax.dynamic_slice_in_dim(spread, offset_cols, slice_width, 1)
    return lax.psum_scatter(
        jnp.dot(own_cols, lm_weight, preferred_element_type=jnp.float32),
        ("gx", "yz"),
        scatter_dimension=0,
        tiled=True,
    )


def attend(queries, k_cache, v_cache, lengths, keys_new, values_new):
    groups = HEADS // KV_HEADS
    factor = 1.0 / math.sqrt(HEAD)
    rows_here = queries.shape[0]
    cache_len = k_cache.shape[1]
    fresh = keys_new.shape[1]
    query_heads = queries.reshape(rows_here, KV_HEADS, groups, HEAD)
    kcache_heads = k_cache.reshape(rows_here, cache_len, KV_HEADS, HEAD)
    vcache_heads = v_cache.reshape(rows_here, cache_len, KV_HEADS, HEAD)
    knew_heads = keys_new.reshape(rows_here, fresh, KV_HEADS, HEAD)
    vnew_heads = values_new.reshape(rows_here, fresh, KV_HEADS, HEAD)
    scores_cache = (
        jnp.einsum("rkgd,rlkd->rkgl", query_heads, kcache_heads, preferred_element_type=jnp.float32)
        * factor
    )
    valid = jnp.arange(cache_len)[None, None, None, :] < lengths[:, None, None, None]
    scores_cache = jnp.where(valid, scores_cache, -jnp.inf)
    scores_new = (
        jnp.einsum("rkgd,rnkd->rkgn", query_heads, knew_heads, preferred_element_type=jnp.float32)
        * factor
    )
    largest = jnp.maximum(jnp.max(scores_cache, -1), jnp.max(scores_new, -1))[..., None]
    exp_cache = jnp.where(valid, jnp.exp(scores_cache - largest), 0.0)
    exp_new = jnp.exp(scores_new - largest)
    denominator = jnp.sum(exp_cache, -1, keepdims=True) + jnp.sum(exp_new, -1, keepdims=True)
    weights_cache = (exp_cache / denominator).astype(jnp.bfloat16)
    weights_new = (exp_new / denominator).astype(jnp.bfloat16)
    result = jnp.einsum(
        "rkgl,rlkd->rkgd", weights_cache, vcache_heads, preferred_element_type=jnp.float32
    )
    result = result + jnp.einsum(
        "rkgn,rnkd->rkgd", weights_new, vnew_heads, preferred_element_type=jnp.float32
    )
    return result.reshape(rows_here, HEADS * HEAD).astype(jnp.bfloat16)


def element_table(token_elem):
    return (token_elem[:, None] == jnp.arange(ELEMENTS, dtype=jnp.int32)[None, :]).astype(
        jnp.float32
    )


def masked_log_probs(logits, remaining, token_elem):
    element_hot = element_table(token_elem)
    per_token = jnp.dot(remaining, element_hot.T)
    allowed = (per_token > 0.5) | (token_elem == ELEMENTS)[None, :]
    largest = jnp.max(jnp.where(allowed, logits, -jnp.inf), -1, keepdims=True)
    shifted = logits - largest
    denominator = jnp.sum(jnp.where(allowed, jnp.exp(shifted), 0.0), -1, keepdims=True)
    return jnp.where(allowed, shifted - jnp.log(denominator), 0.0)


def used_elements(tokens, token_elem):
    token_hot = (tokens[:, None] == jnp.arange(VOCAB, dtype=jnp.int32)[None, :]).astype(jnp.float32)
    return jnp.dot(token_hot, element_table(token_elem))


def per_device(
    hidden_in,
    k_cache,
    v_cache,
    lengths,
    counts,
    token_elem,
    tokens,
    attn_gain,
    qkv_weight,
    o_weight,
    ffn_gain,
    gate_up_weight,
    down_weight,
    final_gain,
    lm_weight,
):
    q_width = HEADS * HEAD
    kv_width = KV_HEADS * HEAD
    key_list = []
    value_list = []
    result_list = []
    logit_steps = []
    for which_step in range(2):
        positions = lengths + which_step
        mixed = project(norm_rows(hidden_in[which_step], attn_gain), qkv_weight)
        queries = rotate(mixed[:, :q_width].reshape(-1, HEADS, HEAD), positions).reshape(
            -1, q_width
        )
        keys_now = rotate(
            mixed[:, q_width : q_width + kv_width].reshape(-1, KV_HEADS, HEAD), positions
        ).reshape(-1, kv_width)
        queries, keys_now, values_now = (queries, keys_now, mixed[:, q_width + kv_width :])
        key_list.append(keys_now)
        value_list.append(values_now)
        attended = attend(
            queries, k_cache, v_cache, lengths, jnp.stack(key_list, 1), jnp.stack(value_list, 1)
        )
        projected = project(attended, o_weight)
        residual = (
            hidden_in[which_step].astype(jnp.float32) + projected.astype(jnp.float32)
        ).astype(jnp.bfloat16)
        gate_up = project(norm_rows(residual, ffn_gain), gate_up_weight)
        hidden_units = (
            jax.nn.silu(gate_up[:, :FF].astype(jnp.float32)) * gate_up[:, FF:].astype(jnp.float32)
        ).astype(jnp.bfloat16)
        lowered = project(hidden_units, down_weight)
        result = (residual.astype(jnp.float32) + lowered.astype(jnp.float32)).astype(jnp.bfloat16)
        logits = head_logits(norm_rows(result, final_gain), lm_weight)
        result, logits = (result, logits)
        result_list.append(result)
        logit_steps.append(logits)
    outputs = jnp.stack(result_list)
    remaining = counts.astype(jnp.float32)
    first_log = masked_log_probs(logit_steps[0], remaining, token_elem)
    remaining = remaining - used_elements(tokens, token_elem)
    second_log = masked_log_probs(logit_steps[1], remaining, token_elem)
    return (outputs, jnp.stack([first_log, second_log]))


def solution(mesh):
    return jax.shard_map(
        per_device,
        mesh=mesh,
        in_specs=(
            P(None, ("gx", "yz"), None),
            P(("gx", "yz"), None, None),
            P(("gx", "yz"), None, None),
            P(("gx", "yz")),
            P(("gx", "yz"), None),
            P(),
            P(("gx", "yz")),
            P(),
            P("gx", "yz"),
            P("gx", "yz"),
            P(),
            P("gx", "yz"),
            P("gx", "yz"),
            P(),
            P(("gx", "yz"), None),
        ),
        out_specs=(P(None, ("gx", "yz"), None), P(None, ("gx", "yz"), None)),
        check_vma=False,
    )
```

profile of v0, /device:TPU:1, one launch (start us, length us, event | category | flops | bytes accessed | tf_op | source)
XLA Modules:
  0.0 964.6 jit_solution(5913646445156775769)
XLA Ops:
  11.1 20.9 %all-gather = bf16[131072]{0:T(1024)(128)(2,1)S(1)} all-gather(bf16[8192]{0:T(1024)(128)(2,1)S(1)} %multiply_convert_fusion.3), channel_id=2, replica_groups=mesh['gx'=8,'yz'=16] {'yz'}, dimensions={0}, use_global_device_ids=true | all-gather | bytes 278528 | tf_op jit(solution)/shard_map/all_gather | solution.py:45
  32.2 16.4 %all_to_all.306 = bf16[16,8,1024]{2,0,1:T(8,128)(2,1)S(1)} all-to-all(bf16[16,8,1024]{2,0,1:T(8,128)(2,1)S(1)} %copy.63), channel_id=1, replica_groups=mesh['gx'=8,'yz'=16] {'gx'}, dimensions={1} | all-to-all | bytes 524288 | tf_op jit(solution)/shard_map/all_to_all | solution.py:46
  50.5 25.7 %reduce-scatter.9.cloned.1.call-done = f32[16,640]{1,0:T(8,128)} async-done(((f32[128,640]{1,0:T(8,128)}), f32[16,640]{1,0:T(8,128)}) %reduce-scatter.9.cloned.1.call-update) | async-done | bytes 40976 | tf_op jit(solution)/shard_map/reduce_scatter | solution.py:51
  78.7 6.8 all-to-all-start.1
  85.5 2.4 copy.97
  94.9 18.7 %all-gather.6 = bf16[16,1,8192]{2,1,0:T(2,128)(2,1)} all-gather(bf16[1,1,8192]{2,1,0:T(2,128)(2,1)S(1)} %reshape.875), channel_id=1, replica_groups=mesh['gx'=8,'yz'=16] {'yz'}, dimensions={0}, use_global_device_ids=true | all-gather | bytes 278528 | tf_op jit(solution)/shard_map/all_gather | solution.py:45
  113.7 3.3 reduce.22
  117.9 18.7 %all_to_all.307 = bf16[16,8,1024]{2,0,1:T(8,128)(2,1)S(1)} all-to-all(bf16[16,8,1024]{2,0,1:T(8,128)(2,1)S(1)} %bitcast.213), channel_id=1, replica_groups=mesh['gx'=8,'yz'=16] {'gx'}, dimensions={1} | all-to-all | bytes 524288 | tf_op jit(solution)/shard_map/all_to_all | solution.py:46
  138.9 25.7 %reduce-scatter.11.cloned.1.call-done = f32[16,512]{1,0:T(8,128)} async-done(((f32[128,512]{1,0:T(8,128)}), f32[16,512]{1,0:T(8,128)}) %reduce-scatter.11.cloned.1.call-update) | async-done | bytes 32784 | tf_op jit(solution)/shard_map/reduce_scatter | solution.py:51
  166.0 13.0 %all_to_all.308 = bf16[16,2,256]{2,1,0:T(2,128)(2,1)S(1)} all-to-all(bf16[16,2,256]{2,1,0:T(2,128)(2,1)S(1)} %reshape.903), channel_id=1, replica_groups=mesh['gx'=8,'yz'=16] {'yz'}, dimensions={0} | all-to-all | bytes 32768 | tf_op jit(solution)/shard_map/all_to_all | solution.py:57
  183.2 18.3 %all-gather.1 = bf16[131072]{0:T(1024)(128)(2,1)} all-gather(bf16[8192]{0:T(1024)(128)(2,1)S(1)} %get-tuple-element.10), channel_id=3, replica_groups=mesh['gx'=8,'yz'=16] {'yz'}, dimensions={0}, use_global_device_ids=true | all-gather | bytes 278528 | tf_op jit(solution)/shard_map/all_gather | solution.py:45
  204.3 18.9 %all_to_all.309 = bf16[16,8,1024]{2,0,1:T(8,128)(2,1)S(1)} all-to-all(bf16[16,8,1024]{2,0,1:T(8,128)(2,1)S(1)} %copy.70), channel_id=1, replica_groups=mesh['gx'=8,'yz'=16] {'gx'}, dimensions={1} | all-to-all | bytes 524288 | tf_op jit(solution)/shard_map/all_to_all | solution.py:46
  223.2 5.5 fusion.105
  228.7 27.9 %reduce-scatter.13.cloned.1.call-done = f32[16,3584]{1,0:T(8,128)} async-done(((f32[128,3584]{1,0:T(8,128)}), f32[16,3584]{1,0:T(8,128)}) %reduce-scatter.13.cloned.1.call-update) | async-done | bytes 229392 | tf_op jit(solution)/shard_map/reduce_scatter | solution.py:51
  261.9 13.7 %all_to_all.310 = bf16[16,2,1792]{2,1,0:T(2,128)(2,1)} all-to-all(bf16[16,2,1792]{2,1,0:T(2,128)(2,1)} %reshape.905), channel_id=1, replica_groups=mesh['gx'=8,'yz'=16] {'yz'}, dimensions={0} | all-to-all | bytes 229376 | tf_op jit(solution)/shard_map/all_to_all | solution.py:57
  278.5 21.8 %all-gather.7 = bf16[16,1,28672]{2,1,0:T(2,128)(2,1)} all-gather(bf16[1,1,28672]{2,1,0:T(2,128)(2,1)S(1)} %convert_bitcast_fusion.2), channel_id=1, replica_groups=mesh['gx'=8,'yz'=16] {'yz'}, dimensions={0}, use_global_device_ids=true | all-gather | bytes 974848 | tf_op jit(solution)/shard_map/all_gather | solution.py:45
  300.3 7.8 reduce.23
  309.5 25.2 %all_to_all.311 = bf16[16,8,3584]{2,0,1:T(8,128)(2,1)S(1)} all-to-all(bf16[16,8,3584]{2,0,1:T(8,128)(2,1)S(1)} %bitcast.204), channel_id=1, replica_groups=mesh['gx'=8,'yz'=16] {'gx'}, dimensions={1} | all-to-all | bytes 1835008 | tf_op jit(solution)/shard_map/all_to_all | solution.py:46
  336.2 25.6 %reduce-scatter.15.cloned.1.call-done = f32[16,512]{1,0:T(8,128)} async-done(((f32[128,512]{1,0:T(8,128)}), f32[16,512]{1,0:T(8,128)}) %reduce-scatter.15.cloned.1.call-update) | async-done | bytes 32784 | tf_op jit(solution)/shard_map/reduce_scatter | solution.py:51
  363.1 13.0 %all_to_all.312 = bf16[16,2,256]{2,1,0:T(2,128)(2,1)S(1)} all-to-all(bf16[16,2,256]{2,1,0:T(2,128)(2,1)S(1)} %reshape.907), channel_id=1, replica_groups=mesh['gx'=8,'yz'=16] {'yz'}, dimensions={0} | all-to-all | bytes 32768 | tf_op jit(solution)/shard_map/all_to_all | solution.py:57
  379.8 18.3 %all-gather.2 = bf16[131072]{0:T(1024)(128)(2,1)} all-gather(bf16[8192]{0:T(1024)(128)(2,1)S(1)} %multiply_convert_fusion.2), channel_id=4, replica_groups=mesh['gx'=8,'yz'=16] {'yz'}, dimensions={0}, use_global_device_ids=true | all-gather | bytes 278528 | tf_op jit(solution)/shard_map/all_gather | solution.py:45
  400.9 18.9 %all_to_all.313 = bf16[16,8,1024]{2,0,1:T(8,128)(2,1)S(1)} all-to-all(bf16[16,8,1024]{2,0,1:T(8,128)(2,1)S(1)} %copy.75), channel_id=1, replica_groups=mesh['gx'=8,'yz'=16] {'gx'}, dimensions={1} | all-to-all | bytes 524288 | tf_op jit(solution)/shard_map/all_to_all | solution.py:46
  421.6 25.1 %reduce-scatter.17.cloned.1.call-done = f32[16,640]{1,0:T(8,128)} async-done(((f32[128,640]{1,0:T(8,128)}), f32[16,640]{1,0:T(8,128)}) %reduce-scatter.17.cloned.1.call-update) | async-done | bytes 40976 | tf_op jit(solution)/shard_map/reduce_scatter | solution.py:51
  451.4 6.9 all-to-all-start.9
  459.0 5.8 all-to-all-done.9
  471.5 16.9 %all-gather.8 = bf16[16,1,8192]{2,1,0:T(2,128)(2,1)S(1)} all-gather(bf16[1,1,8192]{2,1,0:T(2,128)(2,1)S(1)} %reshape.879), channel_id=1, replica_groups=mesh['gx'=8,'yz'=16] {'yz'}, dimensions={0}, use_global_device_ids=true | all-gather | bytes 278528 | tf_op jit(solution)/shard_map/all_gather | solution.py:45
  490.1 18.7 %all_to_all.314 = bf16[16,8,1024]{2,0,1:T(8,128)(2,1)S(1)} all-to-all(bf16[16,8,1024]{2,0,1:T(8,128)(2,1)S(1)} %bitcast.214), channel_id=1, replica_groups=mesh['gx'=8,'yz'=16] {'gx'}, dimensions={1} | all-to-all | bytes 524288 | tf_op jit(solution)/shard_map/all_to_all | solution.py:46
  509.9 25.7 %reduce-scatter.19.cloned.1.call-done = f32[16,512]{1,0:T(8,128)} async-done(((f32[128,512]{1,0:T(8,128)}), f32[16,512]{1,0:T(8,128)}) %reduce-scatter.19.cloned.1.call-update) | async-done | bytes 32784 | tf_op jit(solution)/shard_map/reduce_scatter | solution.py:51
  536.9 13.0 %all_to_all.315 = bf16[16,2,256]{2,1,0:T(2,128)(2,1)S(1)} all-to-all(bf16[16,2,256]{2,1,0:T(2,128)(2,1)S(1)} %reshape.911), channel_id=1, replica_groups=mesh['gx'=8,'yz'=16] {'yz'}, dimensions={0} | all-to-all | bytes 32768 | tf_op jit(solution)/shard_map/all_to_all | solution.py:57
  551.4 16.7 %all-gather.3 = bf16[131072]{0:T(1024)(128)(2,1)S(1)} all-gather(bf16[8192]{0:T(1024)(128)(2,1)S(1)} %get-tuple-element.8), channel_id=5, replica_groups=mesh['gx'=8,'yz'=16] {'yz'}, dimensions={0}, use_global_device_ids=true | all-gather | bytes 278528 | tf_op jit(solution)/shard_map/all_gather | solution.py:45
  568.3 18.6 %all_to_all.316 = bf16[16,8,1024]{2,0,1:T(8,128)(2,1)S(1)} all-to-all(bf16[16,8,1024]{2,0,1:T(8,128)(2,1)S(1)} %copy.84), channel_id=1, replica_groups=mesh['gx'=8,'yz'=16] {'gx'}, dimensions={1} | all-to-all | bytes 524288 | tf_op jit(solution)/shard_map/all_to_all | solution.py:46
  586.9 5.5 fusion.109
  592.4 28.0 %reduce-scatter.21.cloned.1.call-done = f32[16,3584]{1,0:T(8,128)} async-done(((f32[128,3584]{1,0:T(8,128)}), f32[16,3584]{1,0:T(8,128)}) %reduce-scatter.21.cloned.1.call-update) | async-done | bytes 229392 | tf_op jit(solution)/shard_map/reduce_scatter | solution.py:51
  621.9 13.3 %all_to_all.317 = bf16[16,2,1792]{2,1,0:T(2,128)(2,1)S(1)} all-to-all(bf16[16,2,1792]{2,1,0:T(2,128)(2,1)S(1)} %reshape.913), channel_id=1, replica_groups=mesh['gx'=8,'yz'=16] {'yz'}, dimensions={0} | all-to-all | bytes 229376 | tf_op jit(solution)/shard_map/all_to_all | solution.py:57
  635.7 18.4 %all-gather.9 = bf16[16,1,28672]{2,1,0:T(2,128)(2,1)S(1)} all-gather(bf16[1,1,28672]{2,1,0:T(2,128)(2,1)S(1)} %convert_bitcast_fusion), channel_id=1, replica_groups=mesh['gx'=8,'yz'=16] {'yz'}, dimensions={0}, use_global_device_ids=true | all-gather | bytes 974848 | tf_op jit(solution)/shard_map/all_gather | solution.py:45
  654.1 6.5 reduce.25
  662.8 13.4 %all-to-all-start.14 = ((bf16[16,8,3584]{2,0,1:T(8,128)(2,1)}), bf16[16,8,3584]{2,0,1:T(8,128)(2,1)S(1)}, u32[]{:S(2)}, u32[]{:S(2)}) async-start(bf16[16,8,3584]{2,0,1:T(8,128)(2,1)} %bitcast.194), calls=%async_computation.21 | async-start | bytes 1835008 | tf_op jit(solution)/shard_map/all_to_all | solution.py:46
  677.2 12.7 %all-to-all-done.14 = bf16[16,8,3584]{2,0,1:T(8,128)(2,1)S(1)} async-done(((bf16[16,8,3584]{2,0,1:T(8,128)(2,1)}), bf16[16,8,3584]{2,0,1:T(8,128)(2,1)S(1)}, u32[]{:S(2)}, u32[]{:S(2)}) %all-to-all-start.14) | async-done | bytes 917536 | tf_op jit(solution)/shard_map/all_to_all | solution.py:46
  689.9 3.4 fusion.110
  693.7 25.7 %reduce-scatter.23.cloned.1.call-done = f32[16,512]{1,0:T(8,128)} async-done(((f32[128,512]{1,0:T(8,128)}), f32[16,512]{1,0:T(8,128)}) %reduce-scatter.23.cloned.1.call-update) | async-done | bytes 32784 | tf_op jit(solution)/shard_map/reduce_scatter | solution.py:51
  721.3 6.8 all-to-all-start.15
  728.8 5.8 all-to-all-done.15
  736.0 16.7 %all-gather.4 = bf16[131072]{0:T(1024)(128)(2,1)S(1)} all-gather(bf16[8192]{0:T(1024)(128)(2,1)S(1)} %get-tuple-element.21), channel_id=6, replica_groups=mesh['gx'=8,'yz'=16] {'yz'}, dimensions={0}, use_global_device_ids=true | all-gather | bytes 278528 | tf_op jit(solution)/shard_map/all_gather | solution.py:45
  753.7 13.0 %all-to-all-start.16 = ((bf16[16,8,1024]{2,0,1:T(8,128)(2,1)}), bf16[16,8,1024]{2,0,1:T(8,128)(2,1)S(1)}, u32[]{:S(2)}, u32[]{:S(2)}) async-start(bf16[16,8,1024]{2,0,1:T(8,128)(2,1)} %copy.89), calls=%async_computation.24 | async-start | bytes 524288 | tf_op jit(solution)/shard_map/all_to_all | solution.py:46
  766.8 17.9 %all-gather.5 = bf16[131072]{0:T(1024)(128)(2,1)S(1)} all-gather(bf16[8192]{0:T(1024)(128)(2,1)S(1)} %get-tuple-element.22), channel_id=7, replica_groups=mesh['gx'=8,'yz'=16] {'yz'}, dimensions={0}, use_global_device_ids=true | all-gather | bytes 278528 | tf_op jit(solution)/shard_map/all_gather | solution.py:45
  785.6 9.7 %all-to-all-start.17 = ((bf16[16,8,1024]{2,0,1:T(8,128)(2,1)}), bf16[16,8,1024]{2,0,1:T(8,128)(2,1)S(1)}, u32[]{:S(2)}, u32[]{:S(2)}) async-start(bf16[16,8,1024]{2,0,1:T(8,128)(2,1)} %copy.90), calls=%async_computation.25 | async-start | bytes 524288 | tf_op jit(solution)/shard_map/all_to_all | solution.py:46
  796.3 5.5 all-to-all-done.17
  803.5 143.1 %all-reduce.5.cloned.1.call-done = (f32[128,512]{1,0:T(8,128)}, f32[128,512]{1,0:T(8,128)}) async-done(((f32[128,512]{1,0:T(8,128)}, f32[128,512]{1,0:T(8,128)}), (f32[128,512]{1,0:T(8,128)}, f32[128,512]{1,0:T(8,128)})) %all-reduce.5.cloned.1.call-update) | async-done | bytes 524304
  (184 shorter events, 84.4 us)
Async XLA Ops:
  7.2 41.5 %copy-start = (bf16[1024,640]{1,0:T(8,128)(2,1)S(1)}, bf16[1024,640]{1,0:T(8,128)(2,1)}, u32[]{:S(2)}) copy-start(bf16[1024,640]{1,0:T(8,128)(2,1)} %param.23) | copy-start | bytes 3932164
  7.2 69.0 %reduce-scatter.9.cloned.1.call-start = ((), (), s32[]{:S(2)}) async-start(), calls=%async_computation.26 | async-start | bytes 368640 | tf_op jit(solution)/shard_map/reduce_scatter | solution.py:51
  78.7 13.2 %all-to-all-start.1 = ((bf16[16,2,320]{2,1,0:T(2,128)(2,1)}), bf16[16,2,320]{2,1,0:T(2,128)(2,1)S(1)}, u32[]{:S(2)}, u32[]{:S(2)}) async-start(bf16[16,2,320]{2,1,0:T(2,128)(2,1)} %reshape.901), calls=%async_computation.2 | async-start | bytes 49152 | tf_op jit(solution)/shard_map/all_to_all | solution.py:57
  85.4 79.2 %reduce-scatter.11.cloned.1.call-start = ((), (), s32[]{:S(2)}) async-start(), calls=%async_computation.27 | async-start | bytes 294912 | tf_op jit(solution)/shard_map/reduce_scatter | solution.py:51
  85.5 8.8 copy-start.15
  85.5 2.4 copy-start.4
  92.0 2.3 copy-start.5
  92.7 0.6 copy-start.11
  92.7 2.2 copy-start.13
  113.7 66.8 %copy-start.3 = (bf16[2,1,8192]{2,0,1:T(2,128)(2,1)S(1)}, bf16[2,1,8192]{2,0,1:T(2,128)(2,1)}, u32[]{:S(2)}) copy-start(bf16[2,1,8192]{2,0,1:T(2,128)(2,1)} %param.15) | copy-start | bytes 98308
  138.9 117.8 %reduce-scatter.13.cloned.1.call-start = ((), (), s32[]{:S(2)}) async-start(), calls=%async_computation.28 | async-start | bytes 2064384 | tf_op jit(solution)/shard_map/reduce_scatter | solution.py:51
  228.7 133.1 %reduce-scatter.15.cloned.1.call-start = ((), (), s32[]{:S(2)}) async-start(), calls=%async_computation.29 | async-start | bytes 294912 | tf_op jit(solution)/shard_map/reduce_scatter | solution.py:51
  308.1 26.6 %copy-start.1 = (bf16[3584,512]{1,0:T(8,128)(2,1)S(1)}, bf16[3584,512]{1,0:T(8,128)(2,1)}, u32[]{:S(2)}) copy-start(bf16[3584,512]{1,0:T(8,128)(2,1)} %param.27) | copy-start | bytes 11010052
  336.1 110.6 %reduce-scatter.17.cloned.1.call-start = ((), (), s32[]{:S(2)}) async-start(), calls=%async_computation.30 | async-start | bytes 368640 | tf_op jit(solution)/shard_map/reduce_scatter | solution.py:51
  379.8 78.6 %copy-start.12 = (bf16[1,8,64]{2,1,0:T(8,128)(2,1)S(1)}, bf16[1,8,64]{2,1,0:T(8,128)(2,1)}, u32[]{:S(2)}) copy-start(bf16[1,8,64]{2,1,0:T(8,128)(2,1)} %copy-done.11) | copy-start | bytes 3076
  379.8 78.6 %copy-start.14 = (bf16[1,8,64]{2,1,0:T(8,128)(2,1)S(1)}, bf16[1,8,64]{2,1,0:T(8,128)(2,1)}, u32[]{:S(2)}) copy-start(bf16[1,8,64]{2,1,0:T(8,128)(2,1)} %copy-done.13) | copy-start | bytes 3076
  398.1 71.4 %copy-start.16 = (pred[1024]{0:T(1024)(128)(4,1)S(1)}, pred[1024]{0:T(1024)(128)(4,1)}, u32[]{:S(2)}) copy-start(pred[1024]{0:T(1024)(128)(4,1)} %copy-done.15) | copy-start | bytes 3076
  421.0 49.7 %copy-start.17 = (bf16[1,1,8,128]{3,1,2,0:T(2,128)(2,1)S(1)}, bf16[1,1,8,128]{3,1,2,0:T(2,128)(2,1)}, u32[]{:S(2)}) copy-start(bf16[1,1,8,128]{3,1,2,0:T(2,128)(2,1)} %get-tuple-element.12) | copy-start | bytes 6148
  451.4 13.4 %all-to-all-start.9 = ((bf16[16,2,320]{2,1,0:T(2,128)(2,1)}), bf16[16,2,320]{2,1,0:T(2,128)(2,1)}, u32[]{:S(2)}, u32[]{:S(2)}) async-start(bf16[16,2,320]{2,1,0:T(2,128)(2,1)} %reshape.909), calls=%async_computation.14 | async-start | bytes 49152 | tf_op jit(solution)/shard_map/all_to_all | solution.py:57
  458.3 77.3 %reduce-scatter.19.cloned.1.call-start = ((), (), s32[]{:S(2)}) async-start(), calls=%async_computation.31 | async-start | bytes 294912 | tf_op jit(solution)/shard_map/reduce_scatter | solution.py:51
  466.3 4.0 copy-start.18
  466.3 4.7 copy-start.6
  470.9 37.9 %copy-start.2 = (bf16[1024,512]{1,0:T(8,128)(2,1)S(1)}, bf16[1024,512]{1,0:T(8,128)(2,1)}, u32[]{:S(2)}) copy-start(bf16[1024,512]{1,0:T(8,128)(2,1)} %param.24) | copy-start | bytes 3145732
  488.5 62.9 %copy-start.8 = (f32[8192]{0:T(1024)S(1)}, f32[8192]{0:T(1024)}, u32[]{:S(2)}) copy-start(f32[8192]{0:T(1024)} %param.25) | copy-start | bytes 98308
  509.8 110.5 %reduce-scatter.21.cloned.1.call-start = ((), (), s32[]{:S(2)}) async-start(), calls=%async_computation.32 | async-start | bytes 2064384 | tf_op jit(solution)/shard_map/reduce_scatter | solution.py:51
  660.6 16.3 %copy-start.19 = (s32[512]{0:T(512)S(1)}, s32[512]{0:T(512)}, u32[]{:S(2)}) copy-start(s32[512]{0:T(512)} %param.20) | copy-start | bytes 6148
  660.6 16.3 %copy-start.20 = (s32[1,16]{1,0:T(1,128)S(1)}, s32[1,16]{1,0:T(1,128)}, u32[]{:S(2)}) copy-start(s32[1,16]{1,0:T(1,128)} %param.19) | copy-start | bytes 196
  662.8 27.0 %all-to-all-start.14 = ((bf16[16,8,3584]{2,0,1:T(8,128)(2,1)}), bf16[16,8,3584]{2,0,1:T(8,128)(2,1)S(1)}, u32[]{:S(2)}, u32[]{:S(2)}) async-start(bf16[16,8,3584]{2,0,1:T(8,128)(2,1)} %bitcast.194), calls=%async_computation.21 | async-start | bytes 1835008 | tf_op jit(solution)/shard_map/all_to_all | solution.py:46
  676.3 43.1 %reduce-scatter.23.cloned.1.call-start = ((), (), s32[]{:S(2)}) async-start(), calls=%async_computation.33 | async-start | bytes 294912 | tf_op jit(solution)/shard_map/reduce_scatter | solution.py:51
  689.9 46.1 %copy-start.9 = (bf16[8192]{0:T(1024)(128)(2,1)S(1)}, bf16[8192]{0:T(1024)(128)(2,1)}, u32[]{:S(2)}) copy-start(bf16[8192]{0:T(1024)(128)(2,1)} %get-tuple-element.11) | copy-start | bytes 49156
  689.9 46.1 %copy-start.10 = (f32[8192]{0:T(1024)S(1)}, f32[8192]{0:T(1024)}, u32[]{:S(2)}) copy-start(f32[8192]{0:T(1024)} %param.28) | copy-start | bytes 98308
  721.3 13.2 %all-to-all-start.15 = ((bf16[16,2,256]{2,1,0:T(2,128)(2,1)}), bf16[16,2,256]{2,1,0:T(2,128)(2,1)S(1)}, u32[]{:S(2)}, u32[]{:S(2)}) async-start(bf16[16,2,256]{2,1,0:T(2,128)(2,1)} %reshape.915), calls=%async_computation.23 | async-start | bytes 32768 | tf_op jit(solution)/shard_map/all_to_all | solution.py:57
  735.3 60.1 %copy-start.7 = (bf16[64,512]{1,0:T(8,128)(2,1)S(1)}, bf16[64,512]{1,0:T(8,128)(2,1)}, u32[]{:S(2)}) copy-start(bf16[64,512]{1,0:T(8,128)(2,1)} %param.29) | copy-start | bytes 196612
  753.7 32.0 %all-to-all-start.16 = ((bf16[16,8,1024]{2,0,1:T(8,128)(2,1)}), bf16[16,8,1024]{2,0,1:T(8,128)(2,1)S(1)}, u32[]{:S(2)}, u32[]{:S(2)}) async-start(bf16[16,8,1024]{2,0,1:T(8,128)(2,1)} %copy.89), calls=%async_computation.24 | async-start | bytes 524288 | tf_op jit(solution)/shard_map/all_to_all | solution.py:46
  785.6 16.2 %all-to-all-start.17 = ((bf16[16,8,1024]{2,0,1:T(8,128)(2,1)}), bf16[16,8,1024]{2,0,1:T(8,128)(2,1)S(1)}, u32[]{:S(2)}, u32[]{:S(2)}) async-start(bf16[16,8,1024]{2,0,1:T(8,128)(2,1)} %copy.90), calls=%async_computation.25 | async-start | bytes 524288 | tf_op jit(solution)/shard_map/all_to_all | solution.py:46
  795.4 151.2 %all-reduce.5.cloned.1.call-start = ((), (), s32[]{:S(2)}) async-start(), calls=%async_computation.34 | async-start | bytes 1048576
Sparse Core Ops, SparseCore 0:
  49.9 26.2 reduce-scatter.8
  139.0 25.6 reduce-scatter.10
  228.8 27.7 reduce-scatter.12
  336.2 25.5 reduce-scatter.14
  421.1 25.5 reduce-scatter.16
  510.0 25.6 reduce-scatter.18
  592.5 27.7 reduce-scatter.20
  693.4 25.8 reduce-scatter.22
  802.9 143.5 all-reduce.4
where the time goes:
time: 968 us; the launch traced here: 965 us
  blocking collectives  386 us (40%)
  waiting for transfers between devices  384 us (40%)
  other arithmetic  61.6 us (6%)
  starting transfers between devices  56.9 us (6%)
  local copies, waits for them, and re-layouts  27.6 us (3%)
  matrix products  27 us (3%)
  between operations  21.2 us (2%)
    reduce_scatter x8, waiting for transfers between devices, project(): lax.psum_scatter(jnp.dot(spread, weight, preferred_element_type=jnp.float...  209 us
    all_gather x10, blocking collectives, spread_rows(): gathered = lax.all_gather(inputs, 'yz', axis=0, tiled=True)  185 us
    unnamed x10, waiting for transfers between devices  143 us
    all_to_all x7, blocking collectives, spread_rows(): lax.all_to_all(gathered, 'gx', split_axis=1, concat_axis=0, tiled=True)  135 us
    all_to_all x5, blocking collectives, project(): lax.all_to_all(summed.astype(jnp.bfloat16), 'yz', split_axis=0, concat_ax...  66.1 us
    all_to_all x3, starting transfers between devices, spread_rows(): lax.all_to_all(gathered, 'gx', split_axis=1, concat_axis=0, tiled=True)  36.2 us
    dot_general x8, matrix products, project(): jnp.dot(spread, weight, preferred_element_type=jnp.float32)  21.2 us
    all_to_all x3, starting transfers between devices, project(): lax.all_to_all(summed.astype(jnp.bfloat16), 'yz', split_axis=0, concat_ax...  20.4 us
  transfers between devices with their start and end apart: 15, of which 14 were waited for; matrix products, arithmetic and copies ran while one was open for 1% of the time, Pallas kernels for 0%

commit v1 on v0

--- a/solution.py
+++ b/solution.py
@@ -42,7 +42,23 @@
 
 
 def spread_rows(inputs):
-    gathered = lax.all_gather(inputs, "yz", axis=0, tiled=True)
+    count, mine, rows = (lax.axis_size("yz"), lax.axis_index("yz"), inputs.shape[0])
+    upward = [(i, (i + 1) % count) for i in range(count)]
+    left = [(i, (i - 1) % count) for i in range(count)]
+    gathered = jnp.zeros((*inputs.shape[:0], count * rows, *inputs.shape[0 + 1 :]), inputs.dtype)
+    gathered = lax.dynamic_update_slice_in_dim(gathered, inputs, mine * rows, axis=0)
+    from_left = from_right = inputs
+    middle = count // 2
+    for step in range(1, middle + 1):
+        from_left = lax.ppermute(from_left, "yz", upward)
+        gathered = lax.dynamic_update_slice_in_dim(
+            gathered, from_left, (mine - step) % count * rows, axis=0
+        )
+        if step < count - middle:
+            from_right = lax.ppermute(from_right, "yz", left)
+            gathered = lax.dynamic_update_slice_in_dim(
+                gathered, from_right, (mine + step) % count * rows, axis=0
+            )
     return lax.all_to_all(gathered, "gx", split_axis=1, concat_axis=0, tiled=True)
 
 

time: 968 us -> 1440 us (1.49)
  starting transfers between devices: 56.9 us -> 352 us
  local copies, waits for them, and re-layouts: 27.6 us -> 252 us
  blocking collectives: 386 us -> 248 us
  waiting for transfers between devices: 384 us -> 481 us
  other arithmetic: 61.6 us -> 44 us
    ppermute x0 -> x150, starting transfers between devices: none -> 310 us  [the longest x70 297 us: spread_rows(): from_right = lax.ppermute(from_right, 'yz', left)]
    dynamic_update_slice x0 -> x160, local copies, waits for them, and re-layouts: none -> 213 us  [the longest x80 107 us: spread_rows(): lax.dynamic_update_slice_in_dim(gathered, from_left, (mine - step) % coun...]
    all_gather x10 -> x0, blocking collectives: 185 us -> none  [spread_rows(): gathered = lax.all_gather(inputs, 'yz', axis=0, tiled=True)]
    ppermute x0 -> x150, waiting for transfers between devices: none -> 88.3 us  [the longest x80 88 us: spread_rows(): from_left = lax.ppermute(from_left, 'yz', upward)]
    all_to_all x7 -> x8, blocking collectives: 135 us -> 182 us  [spread_rows(): lax.all_to_all(gathered, 'gx', split_axis=1, concat_axis=0, tiled=True)]
    all_gather x4 -> x0, other arithmetic: 19.1 us -> none  [spread_rows(): gathered = lax.all_gather(inputs, 'yz', axis=0, tiled=True)]
    reduce_scatter x8, waiting for transfers between devices: 209 us -> 227 us  [project(): lax.psum_scatter(jnp.dot(spread, weight, preferred_element_type=jnp.float...]
    all_to_all x3 -> x2, starting transfers between devices: 36.2 us -> 21 us  [spread_rows(): lax.all_to_all(gathered, 'gx', split_axis=1, concat_axis=0, tiled=True)]
  transfers between devices with their start and end apart: 15 -> 164, of which waited for: 14 -> 73; matrix products, arithmetic and copies ran while one was open for 1% -> 15% of each run, Pallas kernels for 0% -> 0%
where the time goes in v1:
time: 1440 us; the launch traced here: 1430 us
  waiting for transfers between devices  481 us (33%)
  starting transfers between devices  352 us (24%)
  local copies, waits for them, and re-layouts  252 us (18%)
  blocking collectives  248 us (17%)
  other arithmetic  44 us (3%)
  matrix products  25 us (2%)
  between operations  23.2 us (2%)
    ppermute x70, starting transfers between devices, spread_rows(): from_right = lax.ppermute(from_right, 'yz', left)  297 us
    reduce_scatter x8, waiting for transfers between devices, project(): lax.psum_scatter(jnp.dot(spread, weight, preferred_element_type=jnp.float...  227 us
    all_to_all x8, blocking collectives, spread_rows(): lax.all_to_all(gathered, 'gx', split_axis=1, concat_axis=0, tiled=True)  182 us
    unnamed x10, waiting for transfers between devices  146 us
    dynamic_update_slice x80, local copies, waits for them, and re-layouts, spread_rows(): lax.dynamic_update_slice_in_dim(gathered, from_left, (mine - step) % coun...  107 us
    dynamic_update_slice x70, local copies, waits for them, and re-layouts, spread_rows(): lax.dynamic_update_slice_in_dim(gathered, from_right, (mine + step) % cou...  93.6 us
    ppermute x80, waiting for transfers between devices, spread_rows(): from_left = lax.ppermute(from_left, 'yz', upward)  88 us
    all_to_all x5, blocking collectives, project(): lax.all_to_all(summed.astype(jnp.bfloat16), 'yz', split_axis=0, concat_ax...  66.1 us
  transfers between devices with their start and end apart: 164, of which 73 were waited for; matrix products, arithmetic and copies ran while one was open for 15% of the time, Pallas kernels for 0%

profile of v1, /device:TPU:1, one launch (start us, length us, event | category | flops | bytes accessed | tf_op | source)
XLA Modules:
  0.0 1425.6 jit_solution(6444133985962528771)
XLA Ops:
  13.3 5.0 collective-permute-start.1
  19.5 4.9 collective-permute-start.3
  25.6 4.9 collective-permute-start.5
  31.6 4.9 collective-permute-start.7
  37.7 4.9 collective-permute-start.9
  43.8 4.9 collective-permute-start.11
  49.9 4.9 collective-permute-start.13
  63.9 19.0 %all_to_all.306 = bf16[16,8,1024]{2,0,1:T(8,128)(2,1)S(1)} all-to-all(bf16[16,8,1024]{2,0,1:T(8,128)(2,1)S(1)} %bitcast.236), channel_id=1, replica_groups=mesh['gx'=8,'yz'=16] {'gx'}, dimensions={1} | all-to-all | bytes 524288 | tf_op jit(solution)/shard_map/all_to_all | solution.py:62
  84.7 27.5 %reduce-scatter.9.cloned.1.call-done = f32[16,640]{1,0:T(8,128)} async-done(((f32[128,640]{1,0:T(8,128)}), f32[16,640]{1,0:T(8,128)}) %reduce-scatter.9.cloned.1.call-update) | async-done | bytes 40976 | tf_op jit(solution)/shard_map/reduce_scatter | solution.py:67
  114.7 6.8 all-to-all-start.1
  205.6 21.1 %all_to_all.307 = bf16[16,8,1024]{2,0,1:T(8,128)(2,1)S(1)} all-to-all(bf16[16,8,1024]{2,0,1:T(8,128)(2,1)S(1)} %bitcast.238), channel_id=1, replica_groups=mesh['gx'=8,'yz'=16] {'gx'}, dimensions={1} | all-to-all | bytes 524288 | tf_op jit(solution)/shard_map/all_to_all | solution.py:62
  229.1 28.1 %reduce-scatter.11.cloned.1.call-done = f32[16,512]{1,0:T(8,128)} async-done(((f32[128,512]{1,0:T(8,128)}), f32[16,512]{1,0:T(8,128)}) %reduce-scatter.11.cloned.1.call-update) | async-done | bytes 32784 | tf_op jit(solution)/shard_map/reduce_scatter | solution.py:67
  258.5 13.0 all_to_all.308
  348.2 21.1 %all_to_all.309 = bf16[16,8,1024]{2,0,1:T(8,128)(2,1)S(1)} all-to-all(bf16[16,8,1024]{2,0,1:T(8,128)(2,1)S(1)} %bitcast.240), channel_id=1, replica_groups=mesh['gx'=8,'yz'=16] {'gx'}, dimensions={1} | all-to-all | bytes 524288 | tf_op jit(solution)/shard_map/all_to_all | solution.py:62
  369.3 5.5 fusion.107
  374.9 30.3 %reduce-scatter.13.cloned.1.call-done = f32[16,3584]{1,0:T(8,128)} async-done(((f32[128,3584]{1,0:T(8,128)}), f32[16,3584]{1,0:T(8,128)}) %reduce-scatter.13.cloned.1.call-update) | async-done | bytes 229392 | tf_op jit(solution)/shard_map/reduce_scatter | solution.py:67
  410.5 13.7 all_to_all.310
  534.3 28.6 %all_to_all.311 = bf16[16,8,3584]{2,0,1:T(8,128)(2,1)S(1)} all-to-all(bf16[16,8,3584]{2,0,1:T(8,128)(2,1)S(1)} %bitcast.225), channel_id=1, replica_groups=mesh['gx'=8,'yz'=16] {'gx'}, dimensions={1} | all-to-all | bytes 1835008 | tf_op jit(solution)/shard_map/all_to_all | solution.py:62
  564.3 27.8 %reduce-scatter.15.cloned.1.call-done = f32[16,512]{1,0:T(8,128)} async-done(((f32[128,512]{1,0:T(8,128)}), f32[16,512]{1,0:T(8,128)}) %reduce-scatter.15.cloned.1.call-update) | async-done | bytes 32784 | tf_op jit(solution)/shard_map/reduce_scatter | solution.py:67
  593.5 13.0 all_to_all.312
  682.6 21.2 %all_to_all.313 = bf16[16,8,1024]{2,0,1:T(8,128)(2,1)S(1)} all-to-all(bf16[16,8,1024]{2,0,1:T(8,128)(2,1)S(1)} %bitcast.242), channel_id=1, replica_groups=mesh['gx'=8,'yz'=16] {'gx'}, dimensions={1} | all-to-all | bytes 524288 | tf_op jit(solution)/shard_map/all_to_all | solution.py:62
  705.5 27.5 %reduce-scatter.17.cloned.1.call-done = f32[16,640]{1,0:T(8,128)} async-done(((f32[128,640]{1,0:T(8,128)}), f32[16,640]{1,0:T(8,128)}) %reduce-scatter.17.cloned.1.call-update) | async-done | bytes 40976 | tf_op jit(solution)/shard_map/reduce_scatter | solution.py:67
  737.7 6.9 all-to-all-start.9
  745.4 5.8 all-to-all-done.9
  764.0 4.8 collective-permute-start.78
  770.1 4.8 collective-permute-start.80
  809.3 21.1 %all_to_all.314 = bf16[16,8,1024]{2,0,1:T(8,128)(2,1)S(1)} all-to-all(bf16[16,8,1024]{2,0,1:T(8,128)(2,1)S(1)} %bitcast.244), channel_id=1, replica_groups=mesh['gx'=8,'yz'=16] {'gx'}, dimensions={1} | all-to-all | bytes 524288 | tf_op jit(solution)/shard_map/all_to_all | solution.py:62
  831.6 28.1 %reduce-scatter.19.cloned.1.call-done = f32[16,512]{1,0:T(8,128)} async-done(((f32[128,512]{1,0:T(8,128)}), f32[16,512]{1,0:T(8,128)}) %reduce-scatter.19.cloned.1.call-update) | async-done | bytes 32784 | tf_op jit(solution)/shard_map/reduce_scatter | solution.py:67
  860.9 13.0 all_to_all.315
  926.6 21.1 %all_to_all.316 = bf16[16,8,1024]{2,0,1:T(8,128)(2,1)S(1)} all-to-all(bf16[16,8,1024]{2,0,1:T(8,128)(2,1)S(1)} %bitcast.246), channel_id=1, replica_groups=mesh['gx'=8,'yz'=16] {'gx'}, dimensions={1} | all-to-all | bytes 524288 | tf_op jit(solution)/shard_map/all_to_all | solution.py:62
  947.7 5.5 fusion.111
  953.2 30.3 %reduce-scatter.21.cloned.1.call-done = f32[16,3584]{1,0:T(8,128)} async-done(((f32[128,3584]{1,0:T(8,128)}), f32[16,3584]{1,0:T(8,128)}) %reduce-scatter.21.cloned.1.call-update) | async-done | bytes 229392 | tf_op jit(solution)/shard_map/reduce_scatter | solution.py:67
  985.1 13.4 all_to_all.317
  1005.9 5.0 collective-permute-start.108
  1012.8 5.0 collective-permute-start.110
  1020.6 5.3 collective-permute-start.112
  1028.4 5.2 collective-permute-start.114
  1035.4 5.2 collective-permute-start.116
  1042.3 5.3 collective-permute-start.118
  1089.4 29.0 %all_to_all.318 = bf16[16,8,3584]{2,0,1:T(8,128)(2,1)S(1)} all-to-all(bf16[16,8,3584]{2,0,1:T(8,128)(2,1)S(1)} %bitcast.227), channel_id=1, replica_groups=mesh['gx'=8,'yz'=16] {'gx'}, dimensions={1} | all-to-all | bytes 1835008 | tf_op jit(solution)/shard_map/all_to_all | solution.py:62
  1119.8 27.9 %reduce-scatter.23.cloned.1.call-done = f32[16,512]{1,0:T(8,128)} async-done(((f32[128,512]{1,0:T(8,128)}), f32[16,512]{1,0:T(8,128)}) %reduce-scatter.23.cloned.1.call-update) | async-done | bytes 32784 | tf_op jit(solution)/shard_map/reduce_scatter | solution.py:67
  1149.6 6.8 all-to-all-start.15
  1157.1 5.8 all-to-all-done.15
  1183.8 5.2 collective-permute-start.140
  1223.7 16.2 %all-to-all-start.16 = ((bf16[16,8,1024]{2,0,1:T(8,128)(2,1)}), bf16[16,8,1024]{2,0,1:T(8,128)(2,1)S(1)}, u32[]{:S(2)}, u32[]{:S(2)}) async-start(bf16[16,8,1024]{2,0,1:T(8,128)(2,1)} %bitcast.211), calls=%async_computation.24 | async-start | bytes 524288 | tf_op jit(solution)/shard_map/all_to_all | solution.py:62
  1248.5 4.8 all-to-all-start.17
  1254.3 5.5 all-to-all-done.17
  1261.4 145.7 %all-reduce.5.cloned.1.call-done = (f32[128,512]{1,0:T(8,128)}, f32[128,512]{1,0:T(8,128)}) async-done(((f32[128,512]{1,0:T(8,128)}, f32[128,512]{1,0:T(8,128)}), (f32[128,512]{1,0:T(8,128)}, f32[128,512]{1,0:T(8,128)})) %all-reduce.5.cloned.1.call-update) | async-done | bytes 524304
  (741 shorter events, 631.7 us)
Async XLA Ops:
  7.2 105.0 %reduce-scatter.9.cloned.1.call-start = ((), (), s32[]{:S(2)}) async-start(), calls=%async_computation.26 | async-start | bytes 368640 | tf_op jit(solution)/shard_map/reduce_scatter | solution.py:67
  11.1 8.4 collective-permute-start
  49.9 13.0 collective-permute-start.13
  56.0 7.4 collective-permute-start.14
  114.7 13.2 all-to-all-start.1
  121.5 135.6 %reduce-scatter.11.cloned.1.call-start = ((), (), s32[]{:S(2)}) async-start(), calls=%async_computation.27 | async-start | bytes 294912 | tf_op jit(solution)/shard_map/reduce_scatter | solution.py:67
  171.2 30.1 %collective-permute-start.28 = (bf16[1,8192]{1,0:T(2,128)(2,1)}, bf16[1,8192]{1,0:T(2,128)(2,1)}, u32[]{:S(2)}, u32[]{:S(2)}) collective-permute-start(bf16[1,8192]{1,0:T(2,128)(2,1)} %collective-permute-done.26), channel_id=1, source_target_pairs={{0,15},{1,0},{2,1},{3,2},{4,3},{5,4},{6,5},{7,6},{8,7},{9,8},{10,9... | collective-permute-start | bytes 49160 | tf_op jit(solution)/shard_map/ppermute | solution.py:58
  176.8 26.2 %collective-permute-start.29 = (bf16[1,8192]{1,0:T(2,128)(2,1)}, bf16[1,8192]{1,0:T(2,128)(2,1)}, u32[]{:S(2)}, u32[]{:S(2)}) collective-permute-start(bf16[1,8192]{1,0:T(2,128)(2,1)} %collective-permute-done.27), channel_id=1, source_target_pairs={{0,1},{1,2},{2,3},{3,4},{4,5},{5,6},{6,7},{7,8},{8,9},{9,10},{10,1... | collective-permute-start | bytes 49160 | tf_op jit(solution)/shard_map/ppermute | solution.py:53
  229.1 176.1 %reduce-scatter.13.cloned.1.call-start = ((), (), s32[]{:S(2)}) async-start(), calls=%async_computation.28 | async-start | bytes 2064384 | tf_op jit(solution)/shard_map/reduce_scatter | solution.py:67
  313.8 30.0 %collective-permute-start.43 = (bf16[1,8192]{1,0:T(2,128)(2,1)}, bf16[1,8192]{1,0:T(2,128)(2,1)}, u32[]{:S(2)}, u32[]{:S(2)}) collective-permute-start(bf16[1,8192]{1,0:T(2,128)(2,1)} %collective-permute-done.41), channel_id=1, source_target_pairs={{0,15},{1,0},{2,1},{3,2},{4,3},{5,4},{6,5},{7,6},{8,7},{9,8},{10,9... | collective-permute-start | bytes 49160 | tf_op jit(solution)/shard_map/ppermute | solution.py:58
  319.4 26.1 %collective-permute-start.44 = (bf16[1,8192]{1,0:T(2,128)(2,1)}, bf16[1,8192]{1,0:T(2,128)(2,1)}, u32[]{:S(2)}, u32[]{:S(2)}) collective-permute-start(bf16[1,8192]{1,0:T(2,128)(2,1)} %collective-permute-done.42), channel_id=1, source_target_pairs={{0,1},{1,2},{2,3},{3,4},{4,5},{5,6},{6,7},{7,8},{8,9},{9,10},{10,1... | collective-permute-start | bytes 49160 | tf_op jit(solution)/shard_map/ppermute | solution.py:53
  374.8 217.3 %reduce-scatter.15.cloned.1.call-start = ((), (), s32[]{:S(2)}) async-start(), calls=%async_computation.29 | async-start | bytes 294912 | tf_op jit(solution)/shard_map/reduce_scatter | solution.py:67
  441.1 7.6 collective-permute-start.49
  448.7 8.0 collective-permute-start.51
  449.3 7.3 collective-permute-start.52
  470.6 7.1 collective-permute-start.57
  471.2 54.9 %collective-permute-start.58 = (bf16[1,28672]{1,0:T(2,128)(2,1)}, bf16[1,28672]{1,0:T(2,128)(2,1)}, u32[]{:S(2)}, u32[]{:S(2)}) collective-permute-start(bf16[1,28672]{1,0:T(2,128)(2,1)} %collective-permute-done.56), channel_id=1, source_target_pairs={{0,15},{1,0},{2,1},{3,2},{4,3},{5,4},{6,5},{7,6},{8,7},{9,8},{10,9... | collective-permute-start | bytes 172040 | tf_op jit(solution)/shard_map/ppermute | solution.py:58
  477.6 51.9 %collective-permute-start.59 = (bf16[1,28672]{1,0:T(2,128)(2,1)}, bf16[1,28672]{1,0:T(2,128)(2,1)}, u32[]{:S(2)}, u32[]{:S(2)}) collective-permute-start(bf16[1,28672]{1,0:T(2,128)(2,1)} %collective-permute-done.57), channel_id=1, source_target_pairs={{0,1},{1,2},{2,3},{3,4},{4,5},{5,6},{6,7},{7,8},{8,9},{9,10},{10,1... | collective-permute-start | bytes 172040 | tf_op jit(solution)/shard_map/ppermute | solution.py:53
  564.3 168.7 %reduce-scatter.17.cloned.1.call-start = ((), (), s32[]{:S(2)}) async-start(), calls=%async_computation.30 | async-start | bytes 368640 | tf_op jit(solution)/shard_map/reduce_scatter | solution.py:67
  648.0 30.2 %collective-permute-start.73 = (bf16[1,8192]{1,0:T(2,128)(2,1)}, bf16[1,8192]{1,0:T(2,128)(2,1)}, u32[]{:S(2)}, u32[]{:S(2)}) collective-permute-start(bf16[1,8192]{1,0:T(2,128)(2,1)} %collective-permute-done.71), channel_id=1, source_target_pairs={{0,15},{1,0},{2,1},{3,2},{4,3},{5,4},{6,5},{7,6},{8,7},{9,8},{10,9... | collective-permute-start | bytes 49160 | tf_op jit(solution)/shard_map/ppermute | solution.py:58
  653.6 26.3 %collective-permute-start.74 = (bf16[1,8192]{1,0:T(2,128)(2,1)}, bf16[1,8192]{1,0:T(2,128)(2,1)}, u32[]{:S(2)}, u32[]{:S(2)}) collective-permute-start(bf16[1,8192]{1,0:T(2,128)(2,1)} %collective-permute-done.72), channel_id=1, source_target_pairs={{0,1},{1,2},{2,3},{3,4},{4,5},{5,6},{6,7},{7,8},{8,9},{9,10},{10,1... | collective-permute-start | bytes 49160 | tf_op jit(solution)/shard_map/ppermute | solution.py:53
  737.7 13.5 all-to-all-start.9
  744.6 115.0 %reduce-scatter.19.cloned.1.call-start = ((), (), s32[]{:S(2)}) async-start(), calls=%async_computation.31 | async-start | bytes 294912 | tf_op jit(solution)/shard_map/reduce_scatter | solution.py:67
  795.0 13.3 collective-permute-start.88
  801.1 7.7 collective-permute-start.89
  831.5 152.0 %reduce-scatter.21.cloned.1.call-start = ((), (), s32[]{:S(2)}) async-start(), calls=%async_computation.32 | async-start | bytes 2064384 | tf_op jit(solution)/shard_map/reduce_scatter | solution.py:67
  912.7 12.9 collective-permute-start.103
  918.8 7.3 collective-permute-start.104
  953.2 194.5 %reduce-scatter.23.cloned.1.call-start = ((), (), s32[]{:S(2)}) async-start(), calls=%async_computation.33 | async-start | bytes 294912 | tf_op jit(solution)/shard_map/reduce_scatter | solution.py:67
  1012.8 7.7 collective-permute-start.109
  1012.8 7.8 collective-permute-start.110
  1020.6 7.8 collective-permute-start.111
  1020.6 7.7 collective-permute-start.112
  1042.3 7.1 collective-permute-start.117
  1042.3 41.0 %collective-permute-start.118 = (bf16[1,28672]{1,0:T(2,128)(2,1)}, bf16[1,28672]{1,0:T(2,128)(2,1)}, u32[]{:S(2)}, u32[]{:S(2)}) collective-permute-start(bf16[1,28672]{1,0:T(2,128)(2,1)} %collective-permute-done.116), channel_id=1, source_target_pairs={{0,15},{1,0},{2,1},{3,2},{4,3},{5,4},{6,5},{7,6},{8,7},{9,8},{10,9... | collective-permute-start | bytes 172040 | tf_op jit(solution)/shard_map/ppermute | solution.py:58
  1049.4 36.9 %collective-permute-start.119 = (bf16[1,28672]{1,0:T(2,128)(2,1)}, bf16[1,28672]{1,0:T(2,128)(2,1)}, u32[]{:S(2)}, u32[]{:S(2)}) collective-permute-start(bf16[1,28672]{1,0:T(2,128)(2,1)} %collective-permute-done.117), channel_id=1, source_target_pairs={{0,1},{1,2},{2,3},{3,4},{4,5},{5,6},{6,7},{7,8},{8,9},{9,10},{10,1... | collective-permute-start | bytes 172040 | tf_op jit(solution)/shard_map/ppermute | solution.py:53
  1149.6 13.2 all-to-all-start.15
  1164.7 10.6 collective-permute-start.121
  1183.8 7.1 collective-permute-start.140
  1203.8 12.9 collective-permute-start.146
  1208.6 13.5 collective-permute-start.133
  1208.8 13.2 collective-permute-start.147
  1210.0 12.5 collective-permute-start.134
  1216.7 30.1 %collective-permute-start.148 = (bf16[1,8192]{1,0:T(2,128)(2,1)S(1)}, bf16[1,8192]{1,0:T(2,128)(2,1)S(1)}, u32[]{:S(2)}, u32[]{:S(2)}) collective-permute-start(bf16[1,8192]{1,0:T(2,128)(2,1)S(1)} %collective-permute-done.146), channel_id=1, source_target_pairs={{0,15},{1,0},{2,1},{3,2},{4,3},{5,4},{6,5},{7,6},{8,7},{9,8},{10,9... | collective-permute-start | bytes 49160 | tf_op jit(solution)/shard_map/ppermute | solution.py:58
  1221.9 25.4 %collective-permute-start.149 = (bf16[1,8192]{1,0:T(2,128)(2,1)S(1)}, bf16[1,8192]{1,0:T(2,128)(2,1)S(1)}, u32[]{:S(2)}, u32[]{:S(2)}) collective-permute-start(bf16[1,8192]{1,0:T(2,128)(2,1)S(1)} %collective-permute-done.147), channel_id=1, source_target_pairs={{0,1},{1,2},{2,3},{3,4},{4,5},{5,6},{6,7},{7,8},{8,9},{9,10},{10,1... | collective-permute-start | bytes 49160 | tf_op jit(solution)/shard_map/ppermute | solution.py:53
  1223.7 24.8 %all-to-all-start.16 = ((bf16[16,8,1024]{2,0,1:T(8,128)(2,1)}), bf16[16,8,1024]{2,0,1:T(8,128)(2,1)S(1)}, u32[]{:S(2)}, u32[]{:S(2)}) async-start(bf16[16,8,1024]{2,0,1:T(8,128)(2,1)} %bitcast.211), calls=%async_computation.24 | async-start | bytes 524288 | tf_op jit(solution)/shard_map/all_to_all | solution.py:62
  1248.5 11.3 all-to-all-start.17
  1253.3 153.8 %all-reduce.5.cloned.1.call-start = ((), (), s32[]{:S(2)}) async-start(), calls=%async_computation.34 | async-start | bytes 1048576
  (188 other events, 1939.1 us)
Sparse Core Ops, SparseCore 0:
  84.2 28.0 reduce-scatter.8
  229.2 27.9 reduce-scatter.10
  375.0 30.1 reduce-scatter.12
  564.4 27.7 reduce-scatter.14
  705.0 27.9 reduce-scatter.16
  831.6 27.9 reduce-scatter.18
  953.3 30.1 reduce-scatter.20
  1119.9 27.7 reduce-scatter.22
  1260.9 146.1 all-reduce.4
